TPU v7x, 128 devices: a whole 4x4x4 slice. The times are simulated.
128 devices in a mesh: row: 8 (over y, core), col: 16 (over z, x).
Axes of the slice: x: 4, y: 4, z: 4, core: 2. Of those that a mesh axis runs over, the one named last changes fastest.
Arguments:
- fock: bfloat16 [32768, 16, 2048], P('row', 'col'), may hold values from -6 to 6
- lmo_coef: bfloat16 [32768, 1024], P(('row', 'col')), may hold values from -0.078125 to 0.078125
- three_index: bfloat16 [32768, 512], P(('row', 'col')), may hold values from -6 to 6
- rotation: bfloat16 [16, 8, 1024, 512], P('col', 'row'), may hold values from -0.1875 to 0.1875
- lmo_ids: int32 [16, 8], replicated, may hold values from 0 to 127, as said below
- domains: int32 [128, 8], replicated, may hold values from -1 to 255, as said below
Outputs:
- proj_fock: float32 [16, 8, 512, 512], P('col', 'row')
- three_rot: bfloat16 [16, 8, 512, 512], P('col', 'row')
Inputs may be any that keep to these rules, and one draw needn't show every extreme that they name: `lmo_ids`: every LMO number appears exactly once; row o lists the 8 LMOs owned by column set o. `domains`: entry k of a list is -1 or a block of row panel k; entry 0 is never -1. The present blocks of one list lie in distinct column sets. For one owner o and one entry k, the blocks of the lists of lmo_ids[o, j] over all j lie in distinct column sets; for one j and one entry k, those of lmo_ids[o, j] over all o do too.
All inputs are finite; a program needn't handle non-finite values.
Results may differ from a plain program's by a relative error of at most 0.02.
Values may be sent and summed in bfloat16 or wider, within the bound.
No kernel may reach another device: no remote copies, remote signals or barrier semaphores. Data moves between devices by JAX's collectives and lax.ppermute only.
A program may use at most 192 MiB of HBM per device.

v0:
```python
import jax
import jax.numpy as jnp
from jax import lax
from jax.sharding import PartitionSpec as P

BLK = 128
F32 = jnp.float32
BF16 = jnp.bfloat16


def pick(mask, table):
    return jnp.sum(jnp.where(mask, table, 0), axis=-1)


def body(fock, lmo_coef, three_index, rotation, lmo_ids, domains):
    num_sets = lax.axis_size("col")
    my_row = lax.axis_index("row")
    my_col = lax.axis_index("col")
    dev_rows = lmo_coef.shape[0]
    occ_width = lmo_coef.shape[1]
    dev_blocks = dev_rows // BLK
    dom_blocks = domains.shape[1]
    dom_width = dom_blocks * BLK
    panel_fock = fock[:, 0, :]
    panel_blocks = panel_fock.shape[0] // BLK
    col_blocks = panel_fock.shape[1] // BLK
    doms = jnp.take(domains, lmo_ids, axis=0)
    present = doms >= 0
    clipped = jnp.maximum(doms, 0)
    flat = clipped // dev_blocks
    cset = flat % num_sets
    sub = clipped % dev_blocks
    panel = flat // num_sets
    row_tile = cset * dev_blocks + sub
    col_tile = panel * dev_blocks + sub
    pres_k = lax.dynamic_index_in_dim(present, my_row, 2, keepdims=False)
    cset_k = lax.dynamic_index_in_dim(cset, my_row, 2, keepdims=False)
    sub_k = lax.dynamic_index_in_dim(sub, my_row, 2, keepdims=False)
    rtile_k = lax.dynamic_index_in_dim(row_tile, my_row, 2, keepdims=False)
    mine_k = pres_k & (cset_k == my_col)
    sub_range = jnp.arange(dev_blocks, dtype=jnp.int32)
    sel1 = jnp.any(mine_k[:, :, None] & (sub_k[:, :, None] == sub_range), axis=0).astype(BF16)
    mine2 = present & (cset == my_col)
    has2 = jnp.any(mine2, axis=0)
    rt = pick(
        mine2.transpose(1, 2, 0),
        jnp.broadcast_to(rtile_k.T[:, None, :], mine2.transpose(1, 2, 0).shape),
    )
    ok1 = jnp.any(mine2.transpose(1, 2, 0) & pres_k.T[:, None, :], axis=-1)
    ct = pick(mine2.transpose(1, 2, 0), col_tile.transpose(1, 2, 0))
    fock_tiles = panel_fock.reshape(panel_blocks, BLK, col_blocks, BLK)
    send1_fock = fock_tiles[rt, :, ct, :]
    send1_fock = jnp.where((has2 & ok1)[:, :, None, None], send1_fock, jnp.zeros_like(send1_fock))
    in_rows = jnp.concatenate([lmo_coef, three_index], axis=1).reshape(dev_blocks, BLK, -1)
    send1_rows = jnp.einsum("js,sbw->jbw", sel1, in_rows, preferred_element_type=F32).astype(BF16)
    recv1_rows, recv1_fock = (
        lax.all_to_all(send1_rows, "row", 0, 0, tiled=True),
        lax.all_to_all(send1_fock, "row", 0, 0, tiled=True),
    )
    pres_j = lax.dynamic_index_in_dim(present, my_row, 1, keepdims=False)
    cset_j = lax.dynamic_index_in_dim(cset, my_row, 1, keepdims=False)
    sel2 = (pres_j & (cset_j == my_col)).astype(BF16)
    send2_rows = jnp.einsum("ok,kbw->obw", sel2, recv1_rows, preferred_element_type=F32).astype(
        BF16
    )
    send2_fock = jnp.einsum("ok,akbt->oabt", sel2, recv1_fock, preferred_element_type=F32).astype(
        BF16
    )
    recv2_rows, recv2_fock = (
        lax.all_to_all(send2_rows, "col", 0, 0, tiled=True),
        lax.all_to_all(send2_fock, "col", 0, 0, tiled=True),
    )
    pres_o = lax.dynamic_index_in_dim(pres_j, my_col, 0, keepdims=False)
    cset_o = lax.dynamic_index_in_dim(cset_j, my_col, 0, keepdims=False)
    set_range = jnp.arange(num_sets, dtype=jnp.int32)
    sel3 = (pres_o[:, None] & (cset_o[:, None] == set_range)).astype(BF16)
    rows_dom = jnp.einsum("ks,sbw->kbw", sel3, recv2_rows, preferred_element_type=F32).astype(BF16)
    rows_dom = rows_dom.reshape(dom_width, -1)
    domain_fock = jnp.einsum("ks,sabt->abkt", sel3, recv2_fock, preferred_element_type=F32).astype(
        BF16
    )
    domain_fock = domain_fock.reshape(dom_width, dom_width)
    gathered = lax.all_gather(lmo_coef, "row", axis=0, tiled=True)
    coef_b = lax.psum_scatter(
        jnp.dot(panel_fock, gathered, preferred_element_type=F32).astype(BF16),
        "col",
        scatter_dimension=0,
        tiled=True,
    )
    occ_term = jnp.einsum("ri,rj->ij", lmo_coef, coef_b, preferred_element_type=F32)
    occ_part = lax.psum_scatter(occ_term, ("row", "col"), scatter_dimension=0, tiled=True)
    occ_b = lax.all_gather(occ_part.astype(BF16), ("row", "col"), axis=0, tiled=True)
    fc_blocks = coef_b.reshape(dev_blocks, BLK, occ_width)
    fc1 = jnp.einsum("js,sbw->jbw", sel1, fc_blocks, preferred_element_type=F32).astype(BF16)
    fc1 = lax.all_to_all(fc1, "row", 0, 0, tiled=True)
    fc2 = jnp.einsum("ok,kbw->obw", sel2, fc1, preferred_element_type=F32).astype(BF16)
    fc2 = lax.all_to_all(fc2, "col", 0, 0, tiled=True)
    fc_dom = jnp.einsum("ks,sbw->kbw", sel3, fc2, preferred_element_type=F32).reshape(
        dom_width, occ_width
    )
    coef_dom = rows_dom[:, :occ_width]
    three_dom = rows_dom[:, occ_width:]
    correction = jnp.dot(coef_dom, occ_b, preferred_element_type=F32)
    proj_dom = (fc_dom - 0.5 * correction).astype(BF16)
    slot_rot = rotation[0, 0]
    fock_half = jnp.dot(domain_fock, slot_rot, preferred_element_type=F32).astype(BF16)
    fock_rot = jnp.einsum("xm,xn->mn", slot_rot, fock_half, preferred_element_type=F32)
    coef_rot = jnp.einsum("xm,xi->mi", slot_rot, coef_dom, preferred_element_type=F32).astype(BF16)
    proj_rot = jnp.einsum("xm,xi->mi", slot_rot, proj_dom, preferred_element_type=F32).astype(BF16)
    proj_fock = fock_rot - jnp.einsum("mi,ni->mn", coef_rot, proj_rot, preferred_element_type=F32)
    proj_fock = proj_fock - jnp.einsum("mi,ni->mn", proj_rot, coef_rot, preferred_element_type=F32)
    three_rot = jnp.einsum("xm,xu->mu", slot_rot, three_dom, preferred_element_type=F32).astype(
        BF16
    )
    return (proj_fock[None, None], three_rot[None, None])


def solution(mesh):
    placed = (
        P("row", "col", None),
        P(("row", "col"), None),
        P(("row", "col"), None),
        P("col", "row", None, None),
        P(),
        P(),
    )
    return jax.shard_map(
        body,
        mesh=mesh,
        in_specs=placed,
        out_specs=(P("col", "row", None, None), P("col", "row", None, None)),
        check_vma=False,
    )
```

profile of v0, /device:TPU:1, one launch (start us, length us, event | category | flops | bytes accessed | tf_op | source)
XLA Modules:
  0.0 967.6 jit_solution(5314930313470861836)
XLA Ops:
  8.0 37.6 %all-gather.3.cloned.1.call-done = bf16[2048,1024]{1,0:T(8,128)(2,1)} async-done(((bf16[256,1024]{1,0:T(8,128)(2,1)}), bf16[2048,1024]{1,0:T(8,128)(2,1)}) %all-gather.3.cloned.1.call-update) | async-done | bytes 4194320 | tf_op jit(solution)/shard_map/all_gather | solution.py:83
  45.5 23.4 %fusion.2 = bf16[4096,1024]{1,0:T(8,128)(2,1)} fusion(bf16[2048,1024]{1,0:T(8,128)(2,1)} %all-gather.3.cloned.1.call-done, bf16[4096,1,2048]{2,0,1:T(8,128)(2,1)} %param.6), kind=kOutput, calls=%fused_computation.4 | convolution fusion | flops 17184063488 | bytes 29360128 | tf_op jit(solution)/shard_map/dot_general | solution.py:85
  69.0 9.7 copy.160
  78.6 8.1 copy.130
  88.8 7.4 gather_fusion.1
  96.3 2.7 copy_select_fusion
  99.0 3.9 all-to-all-start
  108.1 21.1 %all-to-all-done = bf16[8,8,128,128]{3,1,2,0:T(8,128)(2,1)S(1)} async-done(((bf16[8,8,128,128]{3,1,2,0:T(8,128)(2,1)}), bf16[8,8,128,128]{3,1,2,0:T(8,128)(2,1)S(1)}, u32[]{:S(2)}, u32[]{:S(2)}) %all-to-all-start) | async-done | bytes 2097184 | tf_op jit(solution)/shard_map/all_to_all | solution.py:58
  129.2 5.5 all-to-all-start.2
  136.3 3.1 copy.132
  139.3 33.0 %all-to-all-done.2 = bf16[8,128,1536]{2,1,0:T(8,128)(2,1)} async-done(((bf16[8,128,1536]{2,1,0:T(8,128)(2,1)}), bf16[8,128,1536]{2,1,0:T(8,128)(2,1)}, u32[]{:S(2)}, u32[]{:S(2)}) %all-to-all-start.2) | async-done | bytes 3145760 | tf_op jit(solution)/shard_map/all_to_all | solution.py:57
  172.3 6.7 all-to-all-start.1
  179.1 3.8 convolution_bitcast_fusion
  182.9 5.4 copy.155
  192.8 51.0 %all-to-all-done.1 = bf16[16,8,128,128]{3,2,1,0:T(8,128)(2,1)} async-done(((bf16[16,8,128,128]{3,2,1,0:T(8,128)(2,1)}), bf16[16,8,128,128]{3,2,1,0:T(8,128)(2,1)}, u32[]{:S(2)}, u32[]{:S(2)}) %all-to-all-start.1) | async-done | bytes 4194336 | tf_op jit(solution)/shard_map/all_to_all | solution.py:71
  243.8 5.8 all-to-all-start.4
  249.6 4.2 convolution_convert_fusion
  253.8 6.2 copy.137
  260.0 15.9 %all-to-all-done.4 = bf16[8,128,1024]{2,1,0:T(8,128)(2,1)S(1)} async-done(((bf16[8,128,1024]{2,1,0:T(8,128)(2,1)}), bf16[8,128,1024]{2,1,0:T(8,128)(2,1)S(1)}, u32[]{:S(2)}, u32[]{:S(2)}) %all-to-all-start.4) | async-done | bytes 2097184 | tf_op jit(solution)/shard_map/all_to_all | solution.py:95
  275.9 4.6 all-to-all-start.3
  282.3 4.3 copy.143
  286.6 90.7 %all-to-all-done.3 = bf16[16,128,1536]{2,1,0:T(8,128)(2,1)} async-done(((bf16[16,128,1536]{2,1,0:T(8,128)(2,1)}), bf16[16,128,1536]{2,1,0:T(8,128)(2,1)}, u32[]{:S(2)}, u32[]{:S(2)}) %all-to-all-start.3) | async-done | bytes 6291488 | tf_op jit(solution)/shard_map/all_to_all | solution.py:70
  377.2 5.2 all-to-all-start.5
  382.7 467.4 %reduce-scatter.7.cloned.1.call-done = f32[8,1024]{1,0:T(8,128)} async-done(((f32[1024,1024]{1,0:T(8,128)}), f32[8,1024]{1,0:T(8,128)}) %reduce-scatter.7.cloned.1.call-update) | async-done | bytes 32784 | tf_op jit(solution)/shard_map/reduce_scatter | solution.py:91
  851.8 4.6 fusion.20
  856.5 2.8 convolution_bitcast_fusion.1
  859.2 6.4 fusion.12
  870.0 2.9 fusion.26
  872.9 4.9 fusion.8
  877.8 4.4 copy.145
  882.2 68.5 %all-gather.5.cloned.1.call-done = bf16[1024,1024]{1,0:T(8,128)(2,1)} async-done(((bf16[8,1024]{1,0:T(8,128)(2,1)}), bf16[1024,1024]{1,0:T(8,128)(2,1)}) %all-gather.5.cloned.1.call-update) | async-done | bytes 2097168 | tf_op jit(solution)/shard_map/all_gather | solution.py:92
  950.7 5.8 fusion.7
  (66 shorter events, 26.4 us)
Async XLA Ops:
  7.2 849.3 %copy-start = (bf16[1,1,1024,512]{3,2,1,0:T(8,128)(2,1)S(1)}, bf16[1,1,1024,512]{3,2,1,0:T(8,128)(2,1)}, u32[]{:S(2)}) copy-start(bf16[1,1,1024,512]{3,2,1,0:T(8,128)(2,1)} %param.9) | copy-start | bytes 3145732
  7.2 38.3 %all-gather.3.cloned.1.call-start = ((), (), s32[]{:S(2)}) async-start(), calls=%async_computation.8 | async-start | bytes 4718592 | tf_op jit(solution)/shard_map/all_gather | solution.py:83
  7.9 171.2 %reduce-scatter.5.cloned.1.call-start = ((), (), s32[]{:S(2)}) async-start(), calls=%async_computation.9 | async-start | bytes 8912896 | tf_op jit(solution)/shard_map/reduce_scatter | solution.py:84
  78.6 8.2 copy-start.7
  78.6 8.3 copy-start.6
  99.0 4.1 copy-start.5
  99.0 30.3 %all-to-all-start = ((bf16[8,8,128,128]{3,1,2,0:T(8,128)(2,1)}), bf16[8,8,128,128]{3,1,2,0:T(8,128)(2,1)S(1)}, u32[]{:S(2)}, u32[]{:S(2)}) async-start(bf16[8,8,128,128]{3,1,2,0:T(8,128)(2,1)} %copy_select_fusion), calls=%async_computation | async-start | bytes 4194304 | tf_op jit(solution)/shard_map/all_to_all | solution.py:58
  129.2 43.1 %all-to-all-start.2 = ((bf16[8,128,1536]{2,1,0:T(8,128)(2,1)}), bf16[8,128,1536]{2,1,0:T(8,128)(2,1)}, u32[]{:S(2)}, u32[]{:S(2)}) async-start(bf16[8,128,1536]{2,1,0:T(8,128)(2,1)} %copy.135), calls=%async_computation.2 | async-start | bytes 6291456 | tf_op jit(solution)/shard_map/all_to_all | solution.py:57
  139.3 39.8 %copy-start.1 = (bf16[256,1024]{1,0:T(8,128)(2,1)S(1)}, bf16[256,1024]{1,0:T(8,128)(2,1)}, u32[]{:S(2)}) copy-start(bf16[256,1024]{1,0:T(8,128)(2,1)} %param.7) | copy-start | bytes 1572868
  172.3 71.5 %all-to-all-start.1 = ((bf16[16,8,128,128]{3,2,1,0:T(8,128)(2,1)}), bf16[16,8,128,128]{3,2,1,0:T(8,128)(2,1)}, u32[]{:S(2)}, u32[]{:S(2)}) async-start(bf16[16,8,128,128]{3,2,1,0:T(8,128)(2,1)} %copy.132), calls=%async_computation.1 | async-start | bytes 8388608 | tf_op jit(solution)/shard_map/all_to_all | solution.py:71
  179.0 671.0 %reduce-scatter.7.cloned.1.call-start = ((), (), s32[]{:S(2)}) async-start(), calls=%async_computation.11 | async-start | bytes 4227072 | tf_op jit(solution)/shard_map/reduce_scatter | solution.py:91
  188.2 1.0 copy-start.2
  243.8 32.1 %all-to-all-start.4 = ((bf16[8,128,1024]{2,1,0:T(8,128)(2,1)}), bf16[8,128,1024]{2,1,0:T(8,128)(2,1)S(1)}, u32[]{:S(2)}, u32[]{:S(2)}) async-start(bf16[8,128,1024]{2,1,0:T(8,128)(2,1)} %copy.141), calls=%async_computation.5 | async-start | bytes 4194304 | tf_op jit(solution)/shard_map/all_to_all | solution.py:95
  275.9 101.3 %all-to-all-start.3 = ((bf16[16,128,1536]{2,1,0:T(8,128)(2,1)}), bf16[16,128,1536]{2,1,0:T(8,128)(2,1)}, u32[]{:S(2)}, u32[]{:S(2)}) async-start(bf16[16,128,1536]{2,1,0:T(8,128)(2,1)} %copy.137), calls=%async_computation.3 | async-start | bytes 12582912 | tf_op jit(solution)/shard_map/all_to_all | solution.py:70
  377.2 495.7 %all-to-all-start.5 = ((bf16[16,128,1024]{2,1,0:T(8,128)(2,1)}), bf16[16,128,1024]{2,1,0:T(8,128)(2,1)}, u32[]{:S(2)}, u32[]{:S(2)}) async-start(bf16[16,128,1024]{2,1,0:T(8,128)(2,1)} %copy.143), calls=%async_computation.6 | async-start | bytes 8388608 | tf_op jit(solution)/shard_map/all_to_all | solution.py:97
  382.4 568.2 %all-gather.5.cloned.1.call-start = ((), (), s32[]{:S(2)}) async-start(), calls=%async_computation.10 | async-start | bytes 2113536 | tf_op jit(solution)/shard_map/all_gather | solution.py:92
  866.5 1.8 copy-start.3
  956.5 1.3 copy-start.4
Sparse Core Ops, SparseCore 0:
  9.7 35.7 all-gather.2
  69.1 83.4 reduce-scatter.4
  188.4 661.6 reduce-scatter.6
  853.3 97.3 all-gather.4
where the time goes:
time: 976 us; the launch traced here: 968 us
  waiting for transfers between devices  786 us (81%)
  matrix products  67.9 us (7%)
  local copies, waits for them, and re-layouts  61.3 us (6%)
  starting transfers between devices  32.1 us (3%)
  between operations  14.5 us (1%)
    reduce_scatter x1, waiting for transfers between devices, body(): lax.psum_scatter(occ_term, ('row', 'col'), scatter_dimension=0, tiled=True)  467 us
    all_to_all x1, waiting for transfers between devices, body(): lax.all_to_all(send2_rows, 'col', 0, 0, tiled=True)  90.7 us
    all_gather x1, waiting for transfers between devices, body(): lax.all_gather(occ_part.astype(BF16), ('row', 'col'), axis=0, tiled=True)  68.5 us
    all_to_all x1, waiting for transfers between devices, body(): lax.all_to_all(send2_fock, 'col', 0, 0, tiled=True)  51 us
    all_gather x1, waiting for transfers between devices, body(): gathered = lax.all_gather(lmo_coef, 'row', axis=0, tiled=True)  37.6 us
    all_to_all x1, waiting for transfers between devices, body(): lax.all_to_all(send1_rows, 'row', 0, 0, tiled=True)  33 us
    dot_general x1, matrix products, body(): jnp.dot(panel_fock, gathered, preferred_element_type=F32).astype(BF16)  23.4 us
    all_to_all x1, waiting for transfers between devices, body(): lax.all_to_all(send1_fock, 'row', 0, 0, tiled=True)  21.1 us
  transfers between devices with their start and end apart: 10, of which 8 were waited for; matrix products, arithmetic and copies ran while one was open for 10% of the time, Pallas kernels for 0%

commit v1 on v0

--- a/solution.py
+++ b/solution.py
@@ -80,7 +80,14 @@
         BF16
     )
     domain_fock = domain_fock.reshape(dom_width, dom_width)
-    gathered = lax.all_gather(lmo_coef, "row", axis=0, tiled=True)
+    world_n = lax.psum(1, "row")
+    gathered = lax.all_to_all(
+        jnp.tile(lmo_coef, [world_n if ix == 0 else 1 for ix in range(lmo_coef.ndim)]),
+        "row",
+        split_axis=0,
+        concat_axis=0,
+        tiled=True,
+    )
     coef_b = lax.psum_scatter(
         jnp.dot(panel_fock, gathered, preferred_element_type=F32).astype(BF16),
         "col",

time: 976 us -> 996 us (1.020)
  blocking collectives: 0 us -> 55.1 us
  waiting for transfers between devices: 786 us -> 748 us
    all_to_all x0 -> x1, blocking collectives: none -> 55.1 us  [body(): lax.all_to_all(jnp.tile(lmo_coef, [world_n if ix == 0 else 1 for ix in ra...]
    all_gather x1 -> x0, waiting for transfers between devices: 37.6 us -> none  [body(): gathered = lax.all_gather(lmo_coef, 'row', axis=0, tiled=True)]
  transfers between devices with their start and end apart: 10 -> 9, of which waited for: 8 -> 7; matrix products, arithmetic and copies ran while one was open for 10% -> 10% of each run, Pallas kernels for 0% -> 0%
where the time goes in v1:
time: 996 us; the launch traced here: 986 us
  waiting for transfers between devices  748 us (75%)
  matrix products  66.7 us (7%)
  local copies, waits for them, and re-layouts  62.9 us (6%)
  blocking collectives  55.1 us (6%)
  starting transfers between devices  33.6 us (3%)
  between operations  14.5 us (1%)
    reduce_scatter x1, waiting for transfers between devices, body(): lax.psum_scatter(occ_term, ('row', 'col'), scatter_dimension=0, tiled=True)  468 us
    all_to_all x1, waiting for transfers between devices, body(): lax.all_to_all(send2_rows, 'col', 0, 0, tiled=True)  90.7 us
    all_gather x1, waiting for transfers between devices, body(): lax.all_gather(occ_part.astype(BF16), ('row', 'col'), axis=0, tiled=True)  68.2 us
    all_to_all x1, blocking collectives, body(): lax.all_to_all(jnp.tile(lmo_coef, [world_n if ix == 0 else 1 for ix in ra...  55.1 us
    all_to_all x1, waiting for transfers between devices, body(): lax.all_to_all(send2_fock, 'col', 0, 0, tiled=True)  51 us
    all_to_all x1, waiting for transfers between devices, body(): lax.all_to_all(send1_rows, 'row', 0, 0, tiled=True)  33 us
    dot_general x1, matrix products, body(): jnp.dot(panel_fock, gathered, preferred_element_type=F32).astype(BF16)  22.2 us
    all_to_all x1, waiting for transfers between devices, body(): lax.all_to_all(send1_fock, 'row', 0, 0, tiled=True)  21 us
  transfers between devices with their start and end apart: 9, of which 7 were waited for; matrix products, arithmetic and copies ran while one was open for 10% of the time, Pallas kernels for 0%

profile of v1, /device:TPU:1, one launch (start us, length us, event | category | flops | bytes accessed | tf_op | source)
XLA Modules:
  0.0 986.5 jit_solution(7304236132089039402)
XLA Ops:
  8.9 55.1 %all_to_all.39 = bf16[8,256,1024]{2,1,0:T(8,128)(2,1)S(1)} all-to-all(bf16[8,256,1024]{2,1,0:T(8,128)(2,1)S(1)} %tile.2), channel_id=1, replica_groups=mesh['row'=8,'col'=16] {'row'}, dimensions={0} | all-to-all | bytes 8388608 | tf_op jit(solution)/shard_map/all_to_all | solution.py:84
  63.9 22.2 %fusion.2 = bf16[4096,1024]{1,0:T(8,128)(2,1)} fusion(bf16[2048,1024]{1,0:T(8,128)(2,1)S(1)} %bitcast.136, bf16[4096,1,2048]{2,0,1:T(8,128)(2,1)} %param.6), kind=kOutput, calls=%fused_computation.4 | convolution fusion | flops 17184063488 | bytes 29360128 | tf_op jit(solution)/shard_map/dot_general | solution.py:92
  86.1 9.7 copy.160
  95.8 8.2 copy.130
  106.0 7.4 gather_fusion.1
  113.5 2.7 copy_select_fusion
  116.2 4.7 all-to-all-start
  126.2 21.0 %all-to-all-done = bf16[8,8,128,128]{3,1,2,0:T(8,128)(2,1)S(1)} async-done(((bf16[8,8,128,128]{3,1,2,0:T(8,128)(2,1)}), bf16[8,8,128,128]{3,1,2,0:T(8,128)(2,1)S(1)}, u32[]{:S(2)}, u32[]{:S(2)}) %all-to-all-start) | async-done | bytes 2097184 | tf_op jit(solution)/shard_map/all_to_all | solution.py:58
  147.2 5.5 all-to-all-start.2
  154.3 3.1 copy.132
  157.3 33.0 %all-to-all-done.2 = bf16[8,128,1536]{2,1,0:T(8,128)(2,1)} async-done(((bf16[8,128,1536]{2,1,0:T(8,128)(2,1)}), bf16[8,128,1536]{2,1,0:T(8,128)(2,1)}, u32[]{:S(2)}, u32[]{:S(2)}) %all-to-all-start.2) | async-done | bytes 3145760 | tf_op jit(solution)/shard_map/all_to_all | solution.py:57
  190.3 7.6 all-to-all-start.1
  198.0 3.8 convolution_bitcast_fusion
  201.8 5.4 copy.155
  211.8 51.0 %all-to-all-done.1 = bf16[16,8,128,128]{3,2,1,0:T(8,128)(2,1)} async-done(((bf16[16,8,128,128]{3,2,1,0:T(8,128)(2,1)}), bf16[16,8,128,128]{3,2,1,0:T(8,128)(2,1)}, u32[]{:S(2)}, u32[]{:S(2)}) %all-to-all-start.1) | async-done | bytes 4194336 | tf_op jit(solution)/shard_map/all_to_all | solution.py:71
  262.7 5.8 all-to-all-start.5
  268.5 4.2 convolution_convert_fusion
  272.8 6.1 copy.137
  278.9 16.0 %all-to-all-done.5 = bf16[8,128,1024]{2,1,0:T(8,128)(2,1)S(1)} async-done(((bf16[8,128,1024]{2,1,0:T(8,128)(2,1)}), bf16[8,128,1024]{2,1,0:T(8,128)(2,1)S(1)}, u32[]{:S(2)}, u32[]{:S(2)}) %all-to-all-start.5) | async-done | bytes 2097184 | tf_op jit(solution)/shard_map/all_to_all | solution.py:102
  294.9 4.6 all-to-all-start.3
  301.2 4.3 copy.143
  305.5 90.7 %all-to-all-done.3 = bf16[16,128,1536]{2,1,0:T(8,128)(2,1)} async-done(((bf16[16,128,1536]{2,1,0:T(8,128)(2,1)}), bf16[16,128,1536]{2,1,0:T(8,128)(2,1)}, u32[]{:S(2)}, u32[]{:S(2)}) %all-to-all-start.3) | async-done | bytes 6291488 | tf_op jit(solution)/shard_map/all_to_all | solution.py:70
  396.2 5.1 all-to-all-start.6
  401.6 467.6 %reduce-scatter.7.cloned.1.call-done = f32[8,1024]{1,0:T(8,128)} async-done(((f32[1024,1024]{1,0:T(8,128)}), f32[8,1024]{1,0:T(8,128)}) %reduce-scatter.7.cloned.1.call-update) | async-done | bytes 32784 | tf_op jit(solution)/shard_map/reduce_scatter | solution.py:98
  871.0 4.6 fusion.20
  875.6 2.8 convolution_bitcast_fusion.1
  878.4 6.4 fusion.12
  889.1 2.9 fusion.26
  892.0 4.9 fusion.8
  896.9 4.4 copy.145
  901.3 68.2 %all-gather.2.cloned.1.call-done = bf16[1024,1024]{1,0:T(8,128)(2,1)} async-done(((bf16[8,1024]{1,0:T(8,128)(2,1)}), bf16[1024,1024]{1,0:T(8,128)(2,1)}) %all-gather.2.cloned.1.call-update) | async-done | bytes 2097168 | tf_op jit(solution)/shard_map/all_gather | solution.py:99
  969.5 5.8 fusion.7
  (65 shorter events, 27.4 us)
Async XLA Ops:
  7.2 868.4 %copy-start = (bf16[1,1,1024,512]{3,2,1,0:T(8,128)(2,1)S(1)}, bf16[1,1,1024,512]{3,2,1,0:T(8,128)(2,1)}, u32[]{:S(2)}) copy-start(bf16[1,1,1024,512]{3,2,1,0:T(8,128)(2,1)} %param.9) | copy-start | bytes 3145732
  7.2 190.8 %reduce-scatter.5.cloned.1.call-start = ((), (), s32[]{:S(2)}) async-start(), calls=%async_computation.9 | async-start | bytes 8912896 | tf_op jit(solution)/shard_map/reduce_scatter | solution.py:91
  95.8 8.2 copy-start.7
  95.8 8.3 copy-start.6
  116.2 4.8 copy-start.5
  116.2 31.0 %all-to-all-start = ((bf16[8,8,128,128]{3,1,2,0:T(8,128)(2,1)}), bf16[8,8,128,128]{3,1,2,0:T(8,128)(2,1)S(1)}, u32[]{:S(2)}, u32[]{:S(2)}) async-start(bf16[8,8,128,128]{3,1,2,0:T(8,128)(2,1)} %copy_select_fusion), calls=%async_computation | async-start | bytes 4194304 | tf_op jit(solution)/shard_map/all_to_all | solution.py:58
  147.2 43.1 %all-to-all-start.2 = ((bf16[8,128,1536]{2,1,0:T(8,128)(2,1)}), bf16[8,128,1536]{2,1,0:T(8,128)(2,1)}, u32[]{:S(2)}, u32[]{:S(2)}) async-start(bf16[8,128,1536]{2,1,0:T(8,128)(2,1)} %copy.135), calls=%async_computation.2 | async-start | bytes 6291456 | tf_op jit(solution)/shard_map/all_to_all | solution.py:57
  157.3 40.7 %copy-start.1 = (bf16[256,1024]{1,0:T(8,128)(2,1)S(1)}, bf16[256,1024]{1,0:T(8,128)(2,1)}, u32[]{:S(2)}) copy-start(bf16[256,1024]{1,0:T(8,128)(2,1)} %param.7) | copy-start | bytes 1572868
  190.3 72.4 %all-to-all-start.1 = ((bf16[16,8,128,128]{3,2,1,0:T(8,128)(2,1)}), bf16[16,8,128,128]{3,2,1,0:T(8,128)(2,1)}, u32[]{:S(2)}, u32[]{:S(2)}) async-start(bf16[16,8,128,128]{3,2,1,0:T(8,128)(2,1)} %copy.132), calls=%async_computation.1 | async-start | bytes 8388608 | tf_op jit(solution)/shard_map/all_to_all | solution.py:71
  198.0 671.2 %reduce-scatter.7.cloned.1.call-start = ((), (), s32[]{:S(2)}) async-start(), calls=%async_computation.11 | async-start | bytes 4227072 | tf_op jit(solution)/shard_map/reduce_scatter | solution.py:98
  207.2 1.0 copy-start.2
  262.7 32.2 %all-to-all-start.5 = ((bf16[8,128,1024]{2,1,0:T(8,128)(2,1)}), bf16[8,128,1024]{2,1,0:T(8,128)(2,1)S(1)}, u32[]{:S(2)}, u32[]{:S(2)}) async-start(bf16[8,128,1024]{2,1,0:T(8,128)(2,1)} %copy.141), calls=%async_computation.6 | async-start | bytes 4194304 | tf_op jit(solution)/shard_map/all_to_all | solution.py:102
  294.9 101.4 %all-to-all-start.3 = ((bf16[16,128,1536]{2,1,0:T(8,128)(2,1)}), bf16[16,128,1536]{2,1,0:T(8,128)(2,1)}, u32[]{:S(2)}, u32[]{:S(2)}) async-start(bf16[16,128,1536]{2,1,0:T(8,128)(2,1)} %copy.137), calls=%async_computation.3 | async-start | bytes 12582912 | tf_op jit(solution)/shard_map/all_to_all | solution.py:70
  396.2 495.8 %all-to-all-start.6 = ((bf16[16,128,1024]{2,1,0:T(8,128)(2,1)}), bf16[16,128,1024]{2,1,0:T(8,128)(2,1)}, u32[]{:S(2)}, u32[]{:S(2)}) async-start(bf16[16,128,1024]{2,1,0:T(8,128)(2,1)} %copy.143), calls=%async_computation.7 | async-start | bytes 8388608 | tf_op jit(solution)/shard_map/all_to_all | solution.py:104
  401.3 568.2 %all-gather.2.cloned.1.call-start = ((), (), s32[]{:S(2)}) async-start(), calls=%async_computation.10 | async-start | bytes 2113536 | tf_op jit(solution)/shard_map/all_gather | solution.py:99
  885.7 1.7 copy-start.3
  975.3 1.3 copy-start.4
Sparse Core Ops, SparseCore 0:
  86.3 84.7 reduce-scatter.4
  207.3 661.8 reduce-scatter.6
  872.6 96.8 all-gather.1
